TPU v7x, 512 devices: a whole 4x8x8 slice. The times are simulated.
512 devices in a mesh: dp: 128 (over y, z, core), owner: 4 (over x).
Axes of the slice: x: 4, y: 8, z: 8, core: 2. Of those that a mesh axis runs over, the one named last changes fastest.
Arguments:
- embeddings: bfloat16 [65536, 1024], P(('dp', 'owner')), may hold values from -120 to 120
- assignment: int32 [65536], P(('dp', 'owner')), may hold values from 0 to 8191, as said below
- pair_list: int32 [8192], replicated, may hold values from 0 to 8191, as said below
Outputs:
- best_similarity: float32 [65536], P(('dp', 'owner'))
Inputs may be any that keep to these rules, and one draw needn't show every extreme that they name: `assignment`: row r's cluster id is (t * n + o) * 16 + c, where n is the number of owner indices, o the owner index of the device holding row r, t an index of dp and c below 16. Among the rows of one device at most 2 share one t, and on every device exactly 2 rows share some t. pair_list[pair_list[k]] = k for every cluster k; cluster k = (t * n + o) * 16 + c and its partner have the same t and different owner indices o.
All inputs are finite; a program needn't handle non-finite values.
Results may differ from a plain program's by a relative error of at most 0.00053.
Values may be sent and summed in bfloat16 or wider, within the bound.
No kernel may reach another device: no remote copies, remote signals or barrier semaphores. Data moves between devices by JAX's collectives and lax.ppermute only.
A program may use at most 64 MiB of HBM per device.

v0:
```python
import jax
import jax.numpy as jnp
from jax import lax
from jax.sharding import PartitionSpec as P

CPD = 16


def shards(embeddings, assignment, pair_list):
    rows, width = embeddings.shape
    n_dp = lax.axis_size("dp")
    n_owner = lax.axis_size("owner")
    capacity = 2 * rows // n_dp
    slots = capacity * n_dp
    here_owner = lax.axis_index("owner")
    here_dp = lax.axis_index("dp")
    all_ids = lax.all_gather(assignment, ("dp", "owner"), axis=0, tiled=False)
    all_ids = all_ids.reshape(n_dp, n_owner, rows)
    values = embeddings.astype(jnp.float32)
    unit = (values * lax.rsqrt(jnp.sum(values * values, axis=1, keepdims=True) + 1e-06)).astype(
        jnp.bfloat16
    )
    target = assignment // (n_owner * CPD)
    onehot = (target[:, None] == jnp.arange(n_dp, dtype=jnp.int32)[None, :]).astype(jnp.int32)
    slot = jnp.sum(jnp.cumsum(onehot, axis=0) * onehot, axis=1) - 1
    position = target * capacity + slot
    first_id = (here_dp * n_owner + here_owner) * CPD
    partners_mine = lax.dynamic_slice_in_dim(pair_list, first_id, CPD)
    send_rows = jnp.zeros((slots, width), jnp.bfloat16).at[position].set(unit)
    got_rows = lax.all_to_all(
        send_rows.reshape(n_dp, capacity, width), "dp", split_axis=0, concat_axis=0, tiled=True
    )
    mine = got_rows.reshape(slots, width)
    rows_p = lax.all_gather(mine, "owner", axis=0, tiled=True)
    hit = all_ids // (n_owner * CPD) == here_dp
    rank = jnp.cumsum(hit.astype(jnp.int32), axis=2) - 1
    which = hit[:, :, :, None] & (
        rank[:, :, :, None] == jnp.arange(capacity, dtype=jnp.int32)[None, None, None, :]
    )
    filled = jnp.any(which, axis=2)
    table = jnp.sum(jnp.where(which, all_ids[:, :, :, None], 0), axis=2)
    table = jnp.where(filled, table, -1)
    ids_p = jnp.transpose(table, (1, 0, 2)).reshape(n_owner * slots)
    mine_ids = lax.dynamic_slice_in_dim(ids_p, here_owner * slots, slots)
    local = jnp.clip(mine_ids - first_id, 0, CPD - 1)
    picked = local[:, None] == jnp.arange(CPD, dtype=jnp.int32)[None, :]
    partner = jnp.sum(jnp.where(picked, partners_mine[None, :], 0), axis=1)
    scores = lax.dot_general(
        mine, rows_p, (((1,), (1,)), ((), ())), preferred_element_type=jnp.float32
    )
    column = jnp.arange(ids_p.shape[0], dtype=jnp.int32)
    itself = here_owner * slots + jnp.arange(slots, dtype=jnp.int32)
    same = (
        (mine_ids[:, None] == ids_p[None, :])
        & (ids_p[None, :] >= 0)
        & (itself[:, None] != column[None, :])
    )
    related = same | (partner[:, None] == ids_p[None, :])
    best = jnp.maximum(-1.0, jnp.max(jnp.where(related, scores, -1.0), axis=1))
    every_best = lax.all_gather(best, "dp", axis=0, tiled=True)
    back = target * slots + here_dp * capacity + slot
    return jnp.take(every_best, back)


def solution(mesh):
    placed = (P(("dp", "owner"), None), P(("dp", "owner")), P())
    return jax.shard_map(
        shards, mesh=mesh, in_specs=placed, out_specs=P(("dp", "owner")), check_vma=False
    )
```

profile of v0, /device:TPU:1, one launch (start us, length us, event | category | flops | bytes accessed | tf_op | source)
XLA Modules:
  0.0 210.9 jit_solution(3328990106305142735)
XLA Ops:
  6.5 0.0 all-gather.5.cloned.1.call-start
  6.5 0.7 and_select_fusion.1
  7.2 0.1 fusion.16
  7.3 0.2 reduce_window_sum.22
  7.5 0.2 select_reduce_fusion.1
  7.6 1.1 fusion.3
  8.7 0.7 compare_select_fusion.1
  9.4 0.0 copy-start.1
  9.4 1.8 scatter_custom_fusion
  11.2 0.2 reshape.108
  11.4 37.7 %all_to_all.5 = bf16[128,2,1024]{2,1,0:T(2,128)(2,1)S(1)} all-to-all(bf16[128,2,1024]{2,1,0:T(2,128)(2,1)S(1)} %reshape.108), channel_id=1, replica_groups=mesh['dp'=128,'owner'=4] {'dp'}, dimensions={0} | all-to-all | bytes 1048576 | tf_op jit(solution)/shard_map/all_to_all | solution.py:30
  49.1 1.0 reshape.109
  50.1 0.0 all-gather.5.cloned.1.call-update
  50.1 0.0 copy-start
  50.1 0.0 copy-done.1
  50.2 96.7 %all-gather.1 = s32[512,1,128]{2,1,0:T(1,128)S(1)} all-gather(s32[1,1,128]{2,1,0:T(1,128)S(1)} %bitcast.12), channel_id=2, replica_groups=mesh['dp'=128,'owner'=4] {'dp','owner'}, dimensions={0}, use_global_device_ids=true | all-gather | bytes 262656 | tf_op jit(solution)/shard_map/all_gather | solution.py:17
  146.8 0.2 copy.19
  147.0 0.4 fusion.8
  147.4 0.2 copy.23
  147.6 0.1 broadcast_add_fusion
  147.7 0.1 copy.24
  147.9 0.2 fusion.6
  148.1 0.2 select_reduce_fusion
  148.3 0.1 copy.26
  148.5 0.2 reshape.107
  148.7 0.8 dynamic_slice.7
  149.4 0.1 subtract_clamp_fusion
  149.5 0.1 select_reduce_fusion.2
  149.6 0.0 all-gather.5.cloned.1.call-done
  149.6 0.0 copy-done
  149.6 2.6 %fusion = f32[256]{0:T(256)S(1)} fusion(bf16[256,1024]{1,0:T(8,128)(2,1)S(1)} %copy-done, bf16[1024,1024]{1,0:T(8,128)(2,1)} %all-gather.5.cloned.1.call-done, s32[256]{0:T(256)S(1)} %get-tuple-element.9, s32[1024]{0:T(1024)S(1)} %reshape.107, s32[256]{0:T(256)S(1)} %select_reduce_fusion.2, s32[256]{0:T(256)S(1)} %get-tuple-element.6, ...), kind=kOutput, calls=%fused_computation.3 | convolution fusion | flops 538967808 | bytes 2630656 | tf_op jit(solution)/shard_map/dot_general | solution.py:48
  152.3 50.1 %all-gather.2 = f32[128,1,256]{2,1,0:T(1,128)S(1)} all-gather(f32[1,1,256]{2,1,0:T(1,128)S(1)} %bitcast.11), channel_id=1, replica_groups=mesh['dp'=128,'owner'=4] {'dp'}, dimensions={0}, use_global_device_ids=true | all-gather | bytes 132096 | tf_op jit(solution)/shard_map/all_gather | solution.py:60
  202.4 1.1 gather_fusion
  203.6 0.5 and_select_fusion
  (6 shorter events, 0.1 us)
Async XLA Ops:
  6.5 143.1 %all-gather.5.cloned.1.call-start = ((), (), s32[]{:S(2)}) async-start(), calls=%async_computation.1 | async-start | bytes 2621440 | tf_op jit(solution)/shard_map/all_gather | solution.py:34
  9.4 40.7 %copy-start.1 = (s32[128]{0:T(128)S(1)}, s32[128]{0:T(128)}, u32[]{:S(2)}) copy-start(s32[128]{0:T(128)} %param.4) | copy-start | bytes 1540
  50.1 99.5 %copy-start = (bf16[256,1024]{1,0:T(8,128)(2,1)S(1)}, bf16[256,1024]{1,0:T(8,128)(2,1)}, u32[]{:S(2)}) copy-start(bf16[256,1024]{1,0:T(8,128)(2,1)} %reshape.109) | copy-start | bytes 1572868
Sparse Core Ops, SparseCore 0:
  50.3 29.7 all-gather.4
where the time goes:
time: 211 us
  blocking collectives  184 us (87%)
  between operations  13.5 us (6%)
  other arithmetic  6.3 us (3%)
  local copies, waits for them, and re-layouts  3.92 us (2%)
  matrix products  2.64 us (1%)
    all_gather x1, blocking collectives, shards(): all_ids = lax.all_gather(assignment, ('dp', 'owner'), axis=0, tiled=False)  96.7 us
    all_gather x1, blocking collectives, shards(): every_best = lax.all_gather(best, 'dp', axis=0, tiled=True)  50.1 us
    all_to_all x1, blocking collectives, shards(): lax.all_to_all(send_rows.reshape(n_dp, capacity, width), 'dp', split_axis...  37.7 us
  transfers between devices with their start and end apart: 1, of which 0 were waited for; matrix products, arithmetic and copies ran while one was open for 1% of the time, Pallas kernels for 0%

commit v1 on v0

--- a/solution.py
+++ b/solution.py
@@ -2,6 +2,7 @@
 import jax.numpy as jnp
 from jax import lax
 from jax.sharding import PartitionSpec as P
+from jax.lax import all_to_all, psum
 
 CPD = 16
 
@@ -57,7 +58,10 @@
     )
     related = same | (partner[:, None] == ids_p[None, :])
     best = jnp.maximum(-1.0, jnp.max(jnp.where(related, scores, -1.0), axis=1))
-    every_best = lax.all_gather(best, "dp", axis=0, tiled=True)
+    _post_pieces_all = lambda inner_x, bus_axis, dimension_no: jnp.concatenate(
+        all_to_all(jnp.stack([inner_x] * psum(1, bus_axis), 0), bus_axis, 0, 0), axis=dimension_no
+    )
+    every_best = _post_pieces_all(best, "dp", 0)
     back = target * slots + here_dp * capacity + slot
     return jnp.take(every_best, back)
 

time: 211 us -> 183 us (0.87)
  blocking collectives: 184 us -> 134 us
  waiting for transfers between devices: 0.03 us -> 12.2 us
  starting transfers between devices: 0.01 us -> 8.54 us
    all_gather x1 -> x0, blocking collectives: 50.1 us -> none  [shards(): every_best = lax.all_gather(best, 'dp', axis=0, tiled=True)]
    all_to_all x0 -> x1, waiting for transfers between devices: none -> 12.2 us  [shards(): all_to_all(jnp.stack([inner_x] * psum(1, bus_axis), 0), bus_axis, 0, 0)]
    all_to_all x0 -> x1, starting transfers between devices: none -> 8.54 us  [shards(): all_to_all(jnp.stack([inner_x] * psum(1, bus_axis), 0), bus_axis, 0, 0)]
  transfers between devices with their start and end apart: 1 -> 2, of which waited for: 0 -> 1; matrix products, arithmetic and copies ran while one was open for 1% -> 1% of each run, Pallas kernels for 0% -> 0%
where the time goes in v1:
time: 183 us; the launch traced here: 182 us
  blocking collectives  134 us (73%)
  between operations  13.6 us (7%)
  waiting for transfers between devices  12.2 us (7%)
  starting transfers between devices  8.54 us (5%)
  other arithmetic  6.3 us (3%)
  local copies, waits for them, and re-layouts  4.63 us (3%)
  matrix products  2.63 us (1%)
    all_gather x1, blocking collectives, shards(): all_ids = lax.all_gather(assignment, ('dp', 'owner'), axis=0, tiled=False)  96.7 us
    all_to_all x1, blocking collectives, shards(): lax.all_to_all(send_rows.reshape(n_dp, capacity, width), 'dp', split_axis...  37.7 us
    all_to_all x1, waiting for transfers between devices, shards(): all_to_all(jnp.stack([inner_x] * psum(1, bus_axis), 0), bus_axis, 0, 0)  12.2 us
    all_to_all x1, starting transfers between devices, shards(): all_to_all(jnp.stack([inner_x] * psum(1, bus_axis), 0), bus_axis, 0, 0)  8.54 us
  transfers between devices with their start and end apart: 2, of which 1 were waited for; matrix products, arithmetic and copies ran while one was open for 1% of the time, Pallas kernels for 0%

profile of v1, /device:TPU:1, one launch (start us, length us, event | category | flops | bytes accessed | tf_op | source)
XLA Modules:
  0.0 182.3 jit_solution(5512067182219593766)
XLA Ops:
  6.5 0.0 all-gather.4.cloned.1.call-start
  6.5 0.7 and_select_fusion.1
  7.2 0.1 fusion.16
  7.3 0.2 reduce_window_sum.22
  7.5 0.2 select_reduce_fusion.1
  7.6 1.1 fusion.3
  8.7 0.7 compare_select_fusion.1
  9.4 0.0 copy-start.1
  9.4 1.8 scatter_custom_fusion
  11.2 0.2 reshape.118
  11.4 37.7 %all_to_all.11 = bf16[128,2,1024]{2,1,0:T(2,128)(2,1)S(1)} all-to-all(bf16[128,2,1024]{2,1,0:T(2,128)(2,1)S(1)} %reshape.118), channel_id=1, replica_groups=mesh['dp'=128,'owner'=4] {'dp'}, dimensions={0} | all-to-all | bytes 1048576 | tf_op jit(solution)/shard_map/all_to_all | solution.py:31
  49.1 1.0 reshape.119
  50.1 0.0 all-gather.4.cloned.1.call-update
  50.1 0.0 copy-start
  50.1 0.0 copy-done.1
  50.2 96.7 %all-gather.1 = s32[512,1,128]{2,1,0:T(1,128)S(1)} all-gather(s32[1,1,128]{2,1,0:T(1,128)S(1)} %bitcast.10), channel_id=2, replica_groups=mesh['dp'=128,'owner'=4] {'dp','owner'}, dimensions={0}, use_global_device_ids=true | all-gather | bytes 262656 | tf_op jit(solution)/shard_map/all_gather | solution.py:18
  146.8 0.2 copy.19
  147.0 0.4 fusion.8
  147.4 0.2 copy.23
  147.6 0.1 broadcast_add_fusion
  147.7 0.1 copy.24
  147.9 0.2 fusion.6
  148.1 0.2 select_reduce_fusion
  148.3 0.1 copy.26
  148.5 0.2 reshape.117
  148.7 0.8 dynamic_slice.7
  149.4 0.1 subtract_clamp_fusion
  149.5 0.1 select_reduce_fusion.2
  149.6 0.0 all-gather.4.cloned.1.call-done
  149.6 0.0 copy-done
  149.6 2.6 %fusion = f32[256]{0:T(256)S(1)} fusion(bf16[256,1024]{1,0:T(8,128)(2,1)S(1)} %copy-done, bf16[1024,1024]{1,0:T(8,128)(2,1)} %all-gather.4.cloned.1.call-done, s32[256]{0:T(256)S(1)} %get-tuple-element.9, s32[1024]{0:T(1024)S(1)} %reshape.117, s32[256]{0:T(256)S(1)} %select_reduce_fusion.2, s32[256]{0:T(256)S(1)} %get-tuple-element.6, ...), kind=kOutput, calls=%fused_computation.3 | convolution fusion | flops 538967808 | bytes 2630656 | tf_op jit(solution)/shard_map/dot_general | solution.py:49
  152.3 0.7 stack.2
  153.0 8.5 %all-to-all-start.1 = ((f32[128,1,256]{2,1,0:T(1,128)}), f32[128,1,256]{2,1,0:T(1,128)S(1)}, u32[]{:S(2)}, u32[]{:S(2)}) async-start(f32[128,1,256]{2,1,0:T(1,128)} %stack.2), calls=%async_computation.1 | async-start | bytes 262144 | tf_op jit(solution)/shard_map/all_to_all | solution.py:62
  161.6 12.2 %all-to-all-done.1 = f32[128,1,256]{2,1,0:T(1,128)S(1)} async-done(((f32[128,1,256]{2,1,0:T(1,128)}), f32[128,1,256]{2,1,0:T(1,128)S(1)}, u32[]{:S(2)}, u32[]{:S(2)}) %all-to-all-start.1) | async-done | bytes 131104 | tf_op jit(solution)/shard_map/all_to_all | solution.py:62
  173.7 1.1 gather_fusion
  174.9 0.5 and_select_fusion
  (6 shorter events, 0.1 us)
Async XLA Ops:
  6.5 143.1 %all-gather.4.cloned.1.call-start = ((), (), s32[]{:S(2)}) async-start(), calls=%async_computation.2 | async-start | bytes 2621440 | tf_op jit(solution)/shard_map/all_gather | solution.py:35
  9.4 40.7 %copy-start.1 = (s32[128]{0:T(128)S(1)}, s32[128]{0:T(128)}, u32[]{:S(2)}) copy-start(s32[128]{0:T(128)} %param.4) | copy-start | bytes 1540
  50.1 99.5 %copy-start = (bf16[256,1024]{1,0:T(8,128)(2,1)S(1)}, bf16[256,1024]{1,0:T(8,128)(2,1)}, u32[]{:S(2)}) copy-start(bf16[256,1024]{1,0:T(8,128)(2,1)} %reshape.119) | copy-start | bytes 1572868
  153.0 20.8 %all-to-all-start.1 = ((f32[128,1,256]{2,1,0:T(1,128)}), f32[128,1,256]{2,1,0:T(1,128)S(1)}, u32[]{:S(2)}, u32[]{:S(2)}) async-start(f32[128,1,256]{2,1,0:T(1,128)} %stack.2), calls=%async_computation.1 | async-start | bytes 262144 | tf_op jit(solution)/shard_map/all_to_all | solution.py:62
Sparse Core Ops, SparseCore 0:
  50.3 29.7 all-gather.3
